TPU v7x, 256 devices: a whole 4x4x8 slice. The times are simulated.
256 devices in a mesh: cell: 16 (over z, core), energy: 16 (over y, x).
Axes of the slice: x: 4, y: 4, z: 8, core: 2. Of those that a mesh axis runs over, the one named last changes fastest.
Arguments:
- ham_diag: float32 [16, 768, 768], P('cell'), as said below
- couple: float32 [16, 128, 128], P('cell'), as said below
- couple_mask: int32 [16, 2, 2], P('cell'), may hold values from 0 to 1, as said below
- energies: float32 [16], P('energy'), may hold values from -0.02 to 0
- lead_front: float32 [16, 128, 128], P('energy'), as said below
- block_list: int32 [16, 16, 2], P('cell'), may hold values from 0 to 11, as said below
- derivative: float32 [16, 16, 4096], P('cell', 'energy'), may hold values from -0.24 to 0.24
- pair_list: int32 [16, 2], replicated, may hold values from 0 to 15
Outputs:
- local_density: float32 [16, 12288], P('energy', 'cell')
- phonon_self: float32 [16, 16, 16, 4096], P('cell', 'energy')
Inputs may be any that keep to these rules, and one draw needn't show every extreme that they name: Each block is symmetric with diagonal entries between 0.1 and 1.5. For every energy in the range of energies, the block-tridiagonal matrix with diagonal blocks ham_diag[c] - energy I and the masked couplings between cells, with coupled[0] lead_front[e] coupled[0]^T subtracted on the first 128 orbitals of cell 0, is positive definite, so that every shifted block, front and reduced matrix is positive definite. `couple`: with its own cell's couple_mask applied, each coupling has spectral norm at most 0.5. `lead_front`: each matrix is symmetric and positive definite with spectral norm at most 1.7, its diagonal entries in 0.5 to 1.5. `block_list`: entry 0 is the block row and entry 1 the block column of a listed 64-block of the cell; about half of the listed blocks are diagonal blocks. `couple_mask`: 1 keeps a block of the coupling, 0 removes it; the diagonal blocks of every cell are kept. `pair_list`: entry 0 names the energy of the first Green's function block, entry 1 that of the second.
All inputs are finite; a program needn't handle non-finite values.
Results may differ from a plain program's by a relative error of at most 0.0003.
Values sent between devices are 32-bit elements; how exact they have to be, the bound alone decides.
No kernel may reach another device: no remote copies, remote signals or barrier semaphores. Data moves between devices by JAX's collectives and lax.ppermute only.
A program may use at most 64 MiB of HBM per device.

v0:
```python
import jax
import jax.numpy as jnp
from jax import lax
from jax.sharding import PartitionSpec as P

BLK = 64


def passed_along(value, axis, steps):
    count = lax.axis_size(axis)
    first, last = (max(0, -steps), min(count, count - steps))
    return lax.ppermute(value, axis, [(source, source + steps) for source in range(first, last)])


def matmul(left_side, right_side):
    return jnp.matmul(left_side, right_side, precision=lax.Precision.HIGHEST)


def invert(matrix):
    lower_factor = jnp.linalg.cholesky(matrix)
    identity = jnp.eye(matrix.shape[-1], dtype=matrix.dtype)
    return jax.scipy.linalg.cho_solve((lower_factor, True), identity)


def expand_mask(couple, couple_mask):
    cell_count = couple.shape[0]
    mask_width = couple_mask.shape[1]
    shaped = couple.reshape(cell_count, mask_width, BLK, mask_width, BLK)
    return (shaped * couple_mask[:, :, None, :, None].astype(couple.dtype)).reshape(couple.shape)


def front_step(previous, inverses, coupling):
    surface = previous.shape[0]
    factor = matmul(coupling, jnp.linalg.cholesky(previous))
    surface_eye = jnp.eye(surface, dtype=previous.dtype)
    reduced = surface_eye - matmul(factor.T, matmul(inverses[:surface, :surface], factor))
    root_reduced = jnp.linalg.cholesky(reduced)
    edge_rows = matmul(inverses[-surface:, :surface], factor)
    solved = jax.scipy.linalg.cho_solve((root_reduced, True), edge_rows.T)
    fronts = inverses[-surface:, -surface:] + matmul(edge_rows, solved)
    return (fronts, factor, root_reduced)


def finish(inverses, factor, root_reduced):
    surface = factor.shape[0]
    left_cols = matmul(inverses[:, :surface], factor)
    solved = jax.scipy.linalg.cho_solve((root_reduced, True), left_cols.T)
    right_cols = inverses[:, -surface:] + matmul(left_cols, solved[:, -surface:])
    corner = inverses[:surface, :surface] + matmul(left_cols[:surface], solved[:, :surface])
    return (left_cols, solved, right_cols, corner)


def back_step(incoming, right_cols, corner, coupling):
    surface = corner.shape[0]
    edge_rows = right_cols[:surface]
    block_corner = corner + matmul(matmul(edge_rows, incoming), edge_rows.T)
    return matmul(matmul(coupling.T, block_corner), coupling)


def pick_blocks(inverses, left_cols, solved, right_cols, weighted, row_blocks, column_blocks):
    block_count = inverses.shape[0] // BLK
    surface = left_cols.shape[1]
    high = lax.Precision.HIGHEST
    base_block = inverses.reshape(block_count, BLK, block_count, BLK)[
        row_blocks, :, column_blocks, :
    ]
    left_rows = left_cols.reshape(block_count, BLK, surface)[row_blocks]
    solved_cols = jnp.moveaxis(
        jnp.take(solved.reshape(surface, block_count, BLK), column_blocks, axis=1), 1, 0
    )
    weighted_rows = weighted.reshape(block_count, BLK, surface)[row_blocks]
    right_rows = right_cols.reshape(block_count, BLK, surface)[column_blocks]
    result = base_block + jnp.einsum("nis,nsj->nij", left_rows, solved_cols, precision=high)
    result = result + jnp.einsum("nis,njs->nij", weighted_rows, right_rows, precision=high)
    return result.reshape(row_blocks.shape[0], BLK * BLK)


def self_energy(regrouped, derivative, pair_list):
    first_pick = jnp.take(regrouped, pair_list[:, 0], axis=0)
    second_pick = jnp.take(regrouped, pair_list[:, 1], axis=0)
    pair_count = pair_list.shape[0]
    listed = derivative.shape[0]
    first_pick = first_pick.reshape(pair_count, listed, BLK, BLK)
    second_pick = second_pick.reshape(pair_count, listed, BLK, BLK)
    coupling_mat = derivative.reshape(listed, BLK, BLK)
    high = lax.Precision.HIGHEST
    left_side = jnp.einsum("nij,pnjk->pnik", coupling_mat, first_pick, precision=high)
    left_side = jnp.einsum("pnik,nlk->pnil", left_side, coupling_mat, precision=high)
    result = jnp.einsum("pnil,pnml->npim", left_side, second_pick, precision=high)
    return result.reshape(listed, pair_count, BLK * BLK)


def on_device(
    ham_diag, couple, couple_mask, energies, lead_front, block_list, derivative, pair_list
):
    cell_count = lax.axis_size("cell")
    cell_index = lax.axis_index("cell")
    energy_count = energies.shape[0]
    surface = couple.shape[1]
    coupled = expand_mask(couple, couple_mask)[0]
    identity = jnp.eye(ham_diag.shape[1], dtype=ham_diag.dtype)
    inverses = jax.vmap(invert)(ham_diag[0][None] - energies[:, None, None] * identity)
    zeros_stack = jnp.zeros((energy_count, surface, surface), jnp.float32)
    stepper = jax.vmap(front_step, in_axes=(0, 0, None))

    def forward_turn(counter, state_in):
        outgoing, factors, roots = state_in
        incoming = passed_along(outgoing, "cell", 1)
        previous = jnp.where(cell_index == 0, lead_front, incoming)

        def forward_working(operand):
            return stepper(operand, inverses, coupled)

        def forward_waiting(operand):
            return state_in

        return lax.cond(cell_index == counter, forward_working, forward_waiting, previous)

    unused, factors, roots = lax.fori_loop(
        0, cell_count, forward_turn, (zeros_stack, zeros_stack, zeros_stack)
    )
    left_cols, solved, right_cols, corner = jax.vmap(finish)(inverses, factors, roots)
    backer = jax.vmap(back_step, in_axes=(0, 0, 0, None))

    def backward_turn(counter, state_in):
        outgoing, weights = state_in
        incoming = passed_along(outgoing, "cell", -1)

        def backward_working(operand):
            return (backer(operand, right_cols, corner, coupled), operand)

        def backward_waiting(operand):
            return state_in

        return lax.cond(
            cell_index == cell_count - 1 - counter, backward_working, backward_waiting, incoming
        )

    unused, weights = lax.fori_loop(0, cell_count, backward_turn, (zeros_stack, zeros_stack))
    weighted = matmul(right_cols, weights)
    local_density = jnp.diagonal(inverses, axis1=1, axis2=2)
    local_density = local_density + jnp.sum(left_cols * jnp.swapaxes(solved, 1, 2), axis=-1)
    local_density = local_density + jnp.sum(weighted * right_cols, axis=-1)
    picker = jax.vmap(pick_blocks, in_axes=(0, 0, 0, 0, 0, None, None))
    picked = picker(
        inverses, left_cols, solved, right_cols, weighted, block_list[0, :, 0], block_list[0, :, 1]
    )
    regrouped = lax.all_to_all(picked, "energy", split_axis=1, concat_axis=0, tiled=True)
    result = self_energy(regrouped, derivative[0], pair_list)
    return (local_density, result[None])


def solution(mesh):
    placed = (
        P("cell", None, None),
        P("cell", None, None),
        P("cell", None, None),
        P("energy"),
        P("energy", None, None),
        P("cell", None, None),
        P("cell", "energy", None),
        P(),
    )
    return jax.shard_map(
        on_device,
        mesh=mesh,
        in_specs=placed,
        out_specs=(P("energy", "cell"), P("cell", "energy", None, None)),
        check_vma=False,
    )
```

profile of v0, /device:TPU:97, one launch (start us, length us, event | category | flops | bytes accessed | tf_op | source)
XLA Modules:
  0.0 1129.4 jit_solution(3794147539829332200)
XLA Ops:
  12.3 11.7 %custom-call.73 = f32[1,128,128]{2,1,0:T(8,128)S(1)} custom-call(f32[1,128,128]{2,1,0:T(8,128)S(1)} %cholesky.490), custom_call_target="Cholesky" | custom-call | tf_op jit(solution)/shard_map/vmap(jit(cholesky))/cholesky | solution.py:20
  24.2 9.8 custom-call.74
  36.9 11.7 %custom-call.75 = f32[1,128,128]{2,1,0:T(8,128)S(1)} custom-call(f32[1,128,128]{2,1,0:T(8,128)S(1)} %cholesky.494), custom_call_target="Cholesky" | custom-call | tf_op jit(solution)/shard_map/vmap(jit(cholesky))/cholesky | solution.py:20
  49.0 10.1 custom-call.76
  61.5 11.7 %custom-call.77 = f32[1,128,128]{2,1,0:T(8,128)S(1)} custom-call(f32[1,128,128]{2,1,0:T(8,128)S(1)} %cholesky.499), custom_call_target="Cholesky" | custom-call | tf_op jit(solution)/shard_map/vmap(jit(cholesky))/cholesky | solution.py:20
  73.4 9.8 custom-call.78
  85.7 11.9 %custom-call.79 = f32[1,128,128]{2,1,0:T(8,128)S(1)} custom-call(f32[1,128,128]{2,1,0:T(8,128)S(1)} %cholesky.504), custom_call_target="Cholesky" | custom-call | tf_op jit(solution)/shard_map/vmap(jit(cholesky))/cholesky | solution.py:20
  97.7 9.8 custom-call.80
  109.8 11.7 %custom-call.81 = f32[1,128,128]{2,1,0:T(8,128)S(1)} custom-call(f32[1,128,128]{2,1,0:T(8,128)S(1)} %cholesky.509), custom_call_target="Cholesky" | custom-call | tf_op jit(solution)/shard_map/vmap(jit(cholesky))/cholesky | solution.py:20
  121.6 9.8 custom-call.82
  133.5 11.7 %custom-call.83 = f32[1,128,128]{2,1,0:T(8,128)S(1)} custom-call(f32[1,128,128]{2,1,0:T(8,128)S(1)} %fusion.92), custom_call_target="Cholesky" | custom-call | tf_op jit(solution)/shard_map/vmap(jit(cholesky))/cholesky | solution.py:20
  155.7 17.8 %while.36 = (s32[]{:T(128)}, f32[1,768,768]{1,2,0:T(8,128)}, s32[6,2]{0,1:T(2,128)S(1)}, f32[6,1,128,128]{3,2,1,0:T(8,128)S(1)}, s32[]{:T(128)}) while((s32[]{:T(128)}, f32[1,768,768]{1,2,0:T(8,128)}, s32[6,2]{0,1:T(2,128)S(1)}, f32[6,1,128,128]{3,2,1,0:T(8,128)S(1)}, s32[]{:T(128)}) %tuple.131), condition=%wide.while_cond, body=%wide.while_body.sunk | while | flops 2 | bytes 393333 | solution.py:22
  173.5 59.4 %custom-call.84 = f32[1,6,128,128]{2,3,1,0:T(8,128)S(1)} custom-call(f32[1,6,128,128]{3,2,1,0:T(8,128)S(1)} %bitcast.534), custom_call_target="InvertDiagBlocksLowerTriangular" | custom-call | tf_op jit(solution)/shard_map/vmap(jit(_cho_solve))/triangular_solve | solution.py:22
  262.4 552.5 %while.34 = (s32[]{:T(128)}, f32[1,128,128]{2,1,0:T(8,128)S(1)}, f32[1,128,128]{1,2,0:T(8,128)}, f32[1,128,128]{2,1,0:T(8,128)S(1)}, s32[]{:T(128)}, /*index=5*/...) while((s32[]{:T(128)}, f32[1,128,128]{2,1,0:T(8,128)S(1)}, ...), condition=%wide.region_17.19_spmd, body=%wide.region_12.18_spmd.sunk | while | flops 176521472 | bytes 3016968 | solution.py:119
  262.7 5.3 collective-permute-start
  269.4 5.5 collective-permute-start
  276.3 5.5 collective-permute-start
  283.2 5.5 collective-permute-start
  290.1 5.5 collective-permute-start
  297.0 5.5 collective-permute-start
  303.9 5.5 collective-permute-start
  310.8 5.5 collective-permute-start
  316.3 261.5 %collective-permute-done = f32[1,128,128]{1,2,0:T(8,128)S(1)} collective-permute-done((f32[1,128,128]{1,2,0:T(8,128)S(1)}, f32[1,128,128]{1,2,0:T(8,128)S(1)}, u32[]{:S(2)}, u32[]{:S(2)}) %collective-permute-start) | collective-permute-done | bytes 65568 | tf_op jit(solution)/shard_map/while/body/eval_jaxpr/ppermute | solution.py:12
  577.8 41.1 %conditional.4 = ((f32[1,128,128]{2,1,0:T(8,128)S(1)}, f32[1,128,128]{1,2,0:T(8,128)}, f32[1,128,128]{2,1,0:T(8,128)S(1)})) conditional(s32[]{:T(128)} %convert_element_type.57, (f32[1,128,128]{2,1,0:T(8,128)S(1)}, f32[1,128,128]{1,2,0:T(8,128)}, f32[1,128,128]{2,1,0:T(8,128)S(1)}) %tuple.120, (f32[1,768,768]{2,1,0:T(8,128)S(1)}, pred[]{:T(512)}, ...), branch_computations={%region_13.13_spmd, %region_14.17_spmd} | conditional | flops 176521472 | bytes 2623525 | solution.py:117
  577.9 11.7 %custom-call.91 = f32[1,128,128]{2,1,0:T(8,128)S(1)} custom-call(f32[1,128,128]{2,1,0:T(8,128)S(1)} %fusion.20), custom_call_target="Cholesky" | custom-call | tf_op jit(solution)/shard_map/while/body/eval_jaxpr/cond/branch_1_fun/vmap(jit(cholesky))/cholesky | solution.py:34
  595.2 11.7 %custom-call.92 = f32[1,128,128]{2,1,0:T(8,128)S(1)} custom-call(f32[1,128,128]{2,1,0:T(8,128)S(1)} %fusion.9), custom_call_target="Cholesky" | custom-call | tf_op jit(solution)/shard_map/while/body/eval_jaxpr/cond/branch_1_fun/vmap(jit(cholesky))/cholesky | solution.py:37
  608.2 9.8 custom-call.59
  622.3 46.6 %collective-permute-start = (f32[1,128,128]{1,2,0:T(8,128)S(1)}, f32[1,128,128]{1,2,0:T(8,128)S(1)}, u32[]{:S(2)}, u32[]{:S(2)}) collective-permute-start(f32[1,128,128]{1,2,0:T(8,128)S(1)} %copy.125), channel_id=1, source_target_pairs={{0,16},{16,32},{32,48},{48,64},{64,80},{80,96},{96,112},{112,128},... | collective-permute-start | bytes 196616 | tf_op jit(solution)/shard_map/while/body/eval_jaxpr/ppermute | solution.py:12
  670.2 5.5 collective-permute-start
  677.1 38.9 %collective-permute-start = (f32[1,128,128]{1,2,0:T(8,128)S(1)}, f32[1,128,128]{1,2,0:T(8,128)S(1)}, u32[]{:S(2)}, u32[]{:S(2)}) collective-permute-start(f32[1,128,128]{1,2,0:T(8,128)S(1)} %copy.125), channel_id=1, source_target_pairs={{0,16},{16,32},{32,48},{48,64},{64,80},{80,96},{96,112},{112,128},... | collective-permute-start | bytes 196616 | tf_op jit(solution)/shard_map/while/body/eval_jaxpr/ppermute | solution.py:12
  717.5 5.5 collective-permute-start
  724.4 41.8 %collective-permute-start = (f32[1,128,128]{1,2,0:T(8,128)S(1)}, f32[1,128,128]{1,2,0:T(8,128)S(1)}, u32[]{:S(2)}, u32[]{:S(2)}) collective-permute-start(f32[1,128,128]{1,2,0:T(8,128)S(1)} %copy.125), channel_id=1, source_target_pairs={{0,16},{16,32},{32,48},{48,64},{64,80},{80,96},{96,112},{112,128},... | collective-permute-start | bytes 196616 | tf_op jit(solution)/shard_map/while/body/eval_jaxpr/ppermute | solution.py:12
  767.6 5.5 collective-permute-start
  774.5 38.9 %collective-permute-start = (f32[1,128,128]{1,2,0:T(8,128)S(1)}, f32[1,128,128]{1,2,0:T(8,128)S(1)}, u32[]{:S(2)}, u32[]{:S(2)}) collective-permute-start(f32[1,128,128]{1,2,0:T(8,128)S(1)} %copy.125), channel_id=1, source_target_pairs={{0,16},{16,32},{32,48},{48,64},{64,80},{80,96},{96,112},{112,128},... | collective-permute-start | bytes 196616 | tf_op jit(solution)/shard_map/while/body/eval_jaxpr/ppermute | solution.py:12
  816.3 9.8 custom-call.85
  829.4 256.0 %while.35 = (s32[]{:T(128)}, f32[1,128,128]{2,1,0:T(8,128)S(1)}, f32[1,128,128]{2,1,0:T(8,128)S(1)}, s32[]{:T(128)}, f32[1,768,128]{2,1,0:T(8,128)S(1)}, /*index...) while((s32[]{:T(128)}, f32[1,128,128]{2,1,0:T(8,128)S(1)}, ...), condition=%wide.region_22.24_spmd, body=%wide.region_19.23_spmd.sunk | while | flops 100679680 | bytes 1245423 | solution.py:139
  831.3 5.5 collective-permute-done.1
  838.8 41.0 %collective-permute-done.1 = f32[1,128,128]{2,1,0:T(8,128)S(1)} collective-permute-done((f32[1,128,128]{2,1,0:T(8,128)S(1)}, f32[1,128,128]{2,1,0:T(8,128)S(1)}, u32[]{:S(2)}, u32[]{:S(2)}) %collective-permute-start.1) | collective-permute-done | bytes 65568 | tf_op jit(solution)/shard_map/while/body/eval_jaxpr/ppermute | solution.py:12
  881.7 4.9 collective-permute-done.1
  888.5 38.8 %collective-permute-done.1 = f32[1,128,128]{2,1,0:T(8,128)S(1)} collective-permute-done((f32[1,128,128]{2,1,0:T(8,128)S(1)}, f32[1,128,128]{2,1,0:T(8,128)S(1)}, u32[]{:S(2)}, u32[]{:S(2)}) %collective-permute-start.1) | collective-permute-done | bytes 65568 | tf_op jit(solution)/shard_map/while/body/eval_jaxpr/ppermute | solution.py:12
  936.0 41.7 %collective-permute-done.1 = f32[1,128,128]{2,1,0:T(8,128)S(1)} collective-permute-done((f32[1,128,128]{2,1,0:T(8,128)S(1)}, f32[1,128,128]{2,1,0:T(8,128)S(1)}, u32[]{:S(2)}, u32[]{:S(2)}) %collective-permute-start.1) | collective-permute-done | bytes 65568 | tf_op jit(solution)/shard_map/while/body/eval_jaxpr/ppermute | solution.py:12
  979.6 4.9 collective-permute-done.1
  986.4 38.2 %collective-permute-done.1 = f32[1,128,128]{2,1,0:T(8,128)S(1)} collective-permute-done((f32[1,128,128]{2,1,0:T(8,128)S(1)}, f32[1,128,128]{2,1,0:T(8,128)S(1)}, u32[]{:S(2)}, u32[]{:S(2)}) %collective-permute-start.1) | collective-permute-done | bytes 65568 | tf_op jit(solution)/shard_map/while/body/eval_jaxpr/ppermute | solution.py:12
  1026.5 10.3 collective-permute-done.1
  1039.8 4.9 collective-permute-done.1
  1086.6 6.4 copy.92
  1108.8 5.8 all-to-all-start
  1114.6 6.3 gather_fusion
  (290 shorter events, 204.2 us)
Async XLA Ops:
  10.9 1.4 copy-start.3
  107.8 39.1 %copy-start.9 = (s32[1,16,2]{1,2,0:T(2,128)S(1)}, s32[1,16,2]{1,2,0:T(2,128)}, u32[]{:S(2)}) copy-start(s32[1,16,2]{1,2,0:T(2,128)} %param.24) | copy-start | bytes 388
  173.5 62.9 %copy-start = (f32[1,768,768]{1,2,0:T(8,128)S(1)}, f32[1,768,768]{1,2,0:T(8,128)}, u32[]{:S(2)}) copy-start(f32[1,768,768]{1,2,0:T(8,128)} %get-tuple-element.723) | copy-start | bytes 7077892
  235.9 3.7 copy-start.1
  256.3 1.5 copy-start.6
  256.3 1.6 copy-start.10
  258.1 3.6 copy-start.5
  262.7 6.6 collective-permute-start
  269.4 6.8 collective-permute-start
  276.3 6.8 collective-permute-start
  283.2 6.8 collective-permute-start
  290.1 6.8 collective-permute-start
  297.0 6.8 collective-permute-start
  303.9 6.8 collective-permute-start
  310.8 267.0 %collective-permute-start = (f32[1,128,128]{1,2,0:T(8,128)S(1)}, f32[1,128,128]{1,2,0:T(8,128)S(1)}, u32[]{:S(2)}, u32[]{:S(2)}) collective-permute-start(f32[1,128,128]{1,2,0:T(8,128)S(1)} %copy.125), channel_id=1, source_target_pairs={{0,16},{16,32},{32,48},{48,64},{64,80},{80,96},{96,112},{112,128},... | collective-permute-start | bytes 196616 | tf_op jit(solution)/shard_map/while/body/eval_jaxpr/ppermute | solution.py:12
  618.9 3.2 collective-permute-start
  622.3 47.9 %collective-permute-start = (f32[1,128,128]{1,2,0:T(8,128)S(1)}, f32[1,128,128]{1,2,0:T(8,128)S(1)}, u32[]{:S(2)}, u32[]{:S(2)}) collective-permute-start(f32[1,128,128]{1,2,0:T(8,128)S(1)} %copy.125), channel_id=1, source_target_pairs={{0,16},{16,32},{32,48},{48,64},{64,80},{80,96},{96,112},{112,128},... | collective-permute-start | bytes 196616 | tf_op jit(solution)/shard_map/while/body/eval_jaxpr/ppermute | solution.py:12
  670.2 6.8 collective-permute-start
  677.1 40.2 %collective-permute-start = (f32[1,128,128]{1,2,0:T(8,128)S(1)}, f32[1,128,128]{1,2,0:T(8,128)S(1)}, u32[]{:S(2)}, u32[]{:S(2)}) collective-permute-start(f32[1,128,128]{1,2,0:T(8,128)S(1)} %copy.125), channel_id=1, source_target_pairs={{0,16},{16,32},{32,48},{48,64},{64,80},{80,96},{96,112},{112,128},... | collective-permute-start | bytes 196616 | tf_op jit(solution)/shard_map/while/body/eval_jaxpr/ppermute | solution.py:12
  717.5 6.8 collective-permute-start
  724.4 43.1 %collective-permute-start = (f32[1,128,128]{1,2,0:T(8,128)S(1)}, f32[1,128,128]{1,2,0:T(8,128)S(1)}, u32[]{:S(2)}, u32[]{:S(2)}) collective-permute-start(f32[1,128,128]{1,2,0:T(8,128)S(1)} %copy.125), channel_id=1, source_target_pairs={{0,16},{16,32},{32,48},{48,64},{64,80},{80,96},{96,112},{112,128},... | collective-permute-start | bytes 196616 | tf_op jit(solution)/shard_map/while/body/eval_jaxpr/ppermute | solution.py:12
  767.6 6.8 collective-permute-start
  774.5 40.2 %collective-permute-start = (f32[1,128,128]{1,2,0:T(8,128)S(1)}, f32[1,128,128]{1,2,0:T(8,128)S(1)}, u32[]{:S(2)}, u32[]{:S(2)}) collective-permute-start(f32[1,128,128]{1,2,0:T(8,128)S(1)} %copy.125), channel_id=1, source_target_pairs={{0,16},{16,32},{32,48},{48,64},{64,80},{80,96},{96,112},{112,128},... | collective-permute-start | bytes 196616 | tf_op jit(solution)/shard_map/while/body/eval_jaxpr/ppermute | solution.py:12
  827.5 0.8 copy-start.2
  829.4 7.4 collective-permute-start.1
  836.8 43.0 %collective-permute-start.1 = (f32[1,128,128]{2,1,0:T(8,128)S(1)}, f32[1,128,128]{2,1,0:T(8,128)S(1)}, u32[]{:S(2)}, u32[]{:S(2)}) collective-permute-start(f32[1,128,128]{2,1,0:T(8,128)S(1)} %get-tuple-element.701), channel_id=1, source_target_pairs={{16,0},{32,16},{48,32},{64,48},{80,64},{96,80},{112,96},{128,112},... | collective-permute-start | bytes 196616 | tf_op jit(solution)/shard_map/while/body/eval_jaxpr/ppermute | solution.py:12
  879.8 6.8 collective-permute-start.1
  886.6 40.7 %collective-permute-start.1 = (f32[1,128,128]{2,1,0:T(8,128)S(1)}, f32[1,128,128]{2,1,0:T(8,128)S(1)}, u32[]{:S(2)}, u32[]{:S(2)}) collective-permute-start(f32[1,128,128]{2,1,0:T(8,128)S(1)} %get-tuple-element.701), channel_id=1, source_target_pairs={{16,0},{32,16},{48,32},{64,48},{80,64},{96,80},{112,96},{128,112},... | collective-permute-start | bytes 196616 | tf_op jit(solution)/shard_map/while/body/eval_jaxpr/ppermute | solution.py:12
  927.3 6.8 collective-permute-start.1
  934.1 43.6 %collective-permute-start.1 = (f32[1,128,128]{2,1,0:T(8,128)S(1)}, f32[1,128,128]{2,1,0:T(8,128)S(1)}, u32[]{:S(2)}, u32[]{:S(2)}) collective-permute-start(f32[1,128,128]{2,1,0:T(8,128)S(1)} %get-tuple-element.701), channel_id=1, source_target_pairs={{16,0},{32,16},{48,32},{64,48},{80,64},{96,80},{112,96},{128,112},... | collective-permute-start | bytes 196616 | tf_op jit(solution)/shard_map/while/body/eval_jaxpr/ppermute | solution.py:12
  977.7 6.8 collective-permute-start.1
  984.4 40.1 %collective-permute-start.1 = (f32[1,128,128]{2,1,0:T(8,128)S(1)}, f32[1,128,128]{2,1,0:T(8,128)S(1)}, u32[]{:S(2)}, u32[]{:S(2)}) collective-permute-start(f32[1,128,128]{2,1,0:T(8,128)S(1)} %get-tuple-element.701), channel_id=1, source_target_pairs={{16,0},{32,16},{48,32},{64,48},{80,64},{96,80},{112,96},{128,112},... | collective-permute-start | bytes 196616 | tf_op jit(solution)/shard_map/while/body/eval_jaxpr/ppermute | solution.py:12
  1024.5 12.2 %collective-permute-start.1 = (f32[1,128,128]{2,1,0:T(8,128)S(1)}, f32[1,128,128]{2,1,0:T(8,128)S(1)}, u32[]{:S(2)}, u32[]{:S(2)}) collective-permute-start(f32[1,128,128]{2,1,0:T(8,128)S(1)} %get-tuple-element.701), channel_id=1, source_target_pairs={{16,0},{32,16},{48,32},{64,48},{80,64},{96,80},{112,96},{128,112},... | collective-permute-start | bytes 196616 | tf_op jit(solution)/shard_map/while/body/eval_jaxpr/ppermute | solution.py:12
  1037.9 6.8 collective-permute-start.1
  1044.7 6.8 collective-permute-start.1
  1051.4 6.8 collective-permute-start.1
  1058.2 6.8 collective-permute-start.1
  1065.0 6.8 collective-permute-start.1
  1071.8 6.8 collective-permute-start.1
  1078.6 6.8 collective-permute-start.1
  1100.5 5.2 copy-start.4
  1108.8 14.2 %all-to-all-start = ((f32[1,16,4096]{2,0,1:T(1,128)}), f32[1,16,4096]{2,0,1:T(1,128)S(1)}, u32[]{:S(2)}, u32[]{:S(2)}) async-start(f32[1,16,4096]{2,0,1:T(1,128)} %reshape.962), calls=%async_computation | async-start | bytes 524288 | tf_op jit(solution)/shard_map/all_to_all | solution.py:148
  1114.6 7.5 copy-start.7
  1114.6 8.3 copy-start.8
where the time goes:
time: 1140 us; the launch traced here: 1130 us
  waiting for transfers between devices  505 us (44%)
  starting transfers between devices  265 us (23%)
  other arithmetic  236 us (21%)
  local copies, waits for them, and re-layouts  60 us (5%)
  matrix products  55.5 us (5%)
    ppermute x32, waiting for transfers between devices, passed_along(): lax.ppermute(value, axis, [(source, source + steps) for source in range(f...  505 us
    ppermute x32, starting transfers between devices, passed_along(): lax.ppermute(value, axis, [(source, source + steps) for source in range(f...  259 us
    another operation x22, other arithmetic, invert(): lower_factor = jnp.linalg.cholesky(matrix)  123 us
    another operation x3, other arithmetic, invert(): return jax.scipy.linalg.cho_solve((lower_factor, True), identity)  60.9 us
    another operation x22, matrix products, invert(): return jax.scipy.linalg.cho_solve((lower_factor, True), identity)  24.4 us
  transfers between devices with their start and end apart: 33, of which 32 were waited for; matrix products, arithmetic and copies ran while one was open for 1% of the time, Pallas kernels for 0%

commit v1 on v0

v1 whole, which is shorter than its diff:
```python
import jax
import jax.numpy as jnp
from jax import lax
from jax.sharding import PartitionSpec as P

BLK = 64


def passed_along(value, axis, steps):
    count = lax.axis_size(axis)
    first, last = (max(0, -steps), min(count, count - steps))
    return lax.ppermute(value, axis, [(source, source + steps) for source in range(first, last)])


def matmul(left_side, right_side):
    return jnp.matmul(left_side, right_side, precision=lax.Precision.HIGHEST)


def tmat(matrix):
    return jnp.swapaxes(matrix, -1, -2)


def invert(matrix):
    lower_factor = jnp.linalg.cholesky(matrix)
    identity = jnp.eye(matrix.shape[-1], dtype=matrix.dtype)
    return jax.scipy.linalg.cho_solve((lower_factor, True), identity)


def lower_solve(lower_factor, rhs):
    return jax.scipy.linalg.solve_triangular(lower_factor, rhs, lower=True)


def expand_mask(couple, couple_mask):
    cell_count = couple.shape[0]
    mask_width = couple_mask.shape[1]
    shaped = couple.reshape(cell_count, mask_width, BLK, mask_width, BLK)
    return (shaped * couple_mask[:, :, None, :, None].astype(couple.dtype)).reshape(couple.shape)


def combine(left_seg, right_seg):
    p_a, q_a, r_a = left_seg
    p_b, q_b, r_b = right_seg
    surface = r_a.shape[-1]
    eye = jnp.eye(surface, dtype=r_a.dtype)
    root = jnp.linalg.cholesky(r_a)
    root_t = tmat(root)
    lp = matmul(root_t, p_b)
    reduced = eye - matmul(lp, root)
    root_reduced = jnp.linalg.cholesky(reduced)
    rhs = jnp.concatenate([matmul(root_t, q_b), matmul(lp, tmat(q_a))], axis=-1)
    solved = lower_solve(root_reduced, rhs)
    gram = matmul(tmat(solved), solved)
    r_c = r_b + gram[..., :surface, :surface]
    q_c = matmul(q_a, q_b) + gram[..., surface:, :surface]
    p_c = p_a + matmul(matmul(q_a, p_b), tmat(q_a)) + gram[..., surface:, surface:]
    return (p_c, q_c, r_c)


def self_energy(regrouped, derivative, pair_list):
    first_pick = jnp.take(regrouped, pair_list[:, 0], axis=0)
    second_pick = jnp.take(regrouped, pair_list[:, 1], axis=0)
    pair_count = pair_list.shape[0]
    listed = derivative.shape[0]
    first_pick = first_pick.reshape(pair_count, listed, BLK, BLK)
    second_pick = second_pick.reshape(pair_count, listed, BLK, BLK)
    coupling_mat = derivative.reshape(listed, BLK, BLK)
    high = lax.Precision.HIGHEST
    left_side = jnp.einsum("nij,pnjk->pnik", coupling_mat, first_pick, precision=high)
    left_side = jnp.einsum("pnik,nlk->pnil", left_side, coupling_mat, precision=high)
    result = jnp.einsum("pnil,pnml->npim", left_side, second_pick, precision=high)
    return result.reshape(listed, pair_count, BLK * BLK)


def on_device(
    ham_diag, couple, couple_mask, energies, lead_front, block_list, derivative, pair_list
):
    cell_count = lax.axis_size("cell")
    cell_index = lax.axis_index("cell")
    surface = couple.shape[1]
    size = ham_diag.shape[1]
    coupling = expand_mask(couple, couple_mask)[0]
    eye = jnp.eye(surface, dtype=jnp.float32)
    is_first = cell_index == 0
    is_last = cell_index == cell_count - 1

    lead_self = matmul(matmul(coupling, lead_front[0]), coupling.T)
    lead_self = jnp.where(is_first, lead_self, jnp.zeros_like(lead_self))
    shifted = ham_diag[0] - energies[0] * jnp.eye(size, dtype=jnp.float32)
    shifted = shifted.at[:surface, :surface].add(-lead_self)
    inverse = invert(shifted)

    corner = inverse[:surface, :surface]
    leaf = (
        matmul(matmul(coupling.T, corner), coupling),
        matmul(coupling.T, inverse[:surface, -surface:]),
        inverse[-surface:, -surface:],
    )
    prefix = leaf
    suffix = leaf
    distance = 1
    while distance < cell_count:
        from_left = passed_along(prefix, "cell", distance)
        from_right = passed_along(suffix, "cell", -distance)
        has_left = cell_index >= distance
        has_right = cell_index + distance < cell_count
        safe_left = jnp.where(has_left, from_left[2], eye)
        left_segs = tuple(
            jnp.stack([a, b]) for a, b in zip((from_left[0], from_left[1], safe_left), suffix)
        )
        right_segs = tuple(jnp.stack([a, b]) for a, b in zip(prefix, from_right))
        joined = combine(left_segs, right_segs)
        prefix = tuple(jnp.where(has_left, j[0], o) for j, o in zip(joined, prefix))
        suffix = tuple(jnp.where(has_right, j[1], o) for j, o in zip(joined, suffix))
        distance *= 2

    front_before = passed_along(prefix[2], "cell", 1)
    right_self = passed_along(suffix[0], "cell", -1)
    front_before = jnp.where(is_first, eye, front_before)
    right_self = jnp.where(is_last, jnp.zeros_like(right_self), right_self)

    roots = jnp.linalg.cholesky(jnp.stack([front_before, prefix[2]]))
    factor = matmul(coupling, roots[0])
    factor = jnp.where(is_first, jnp.zeros_like(factor), factor)
    root_front = roots[1]
    reduced_left = eye - matmul(matmul(factor.T, corner), factor)
    reduced_right = eye - matmul(matmul(root_front.T, right_self), root_front)
    root_reduced = jnp.linalg.cholesky(jnp.stack([reduced_left, reduced_right]))
    left_cols = matmul(inverse[:, :surface], factor)
    solved_left = lower_solve(root_reduced[0], left_cols.T)
    green = inverse + matmul(solved_left.T, solved_left)
    edge_rows = green[-surface:, :]
    weighted_rows = matmul(right_self, edge_rows)
    solved_right = lower_solve(root_reduced[1], matmul(root_front.T, weighted_rows))
    full = green + matmul(edge_rows.T, weighted_rows) + matmul(solved_right.T, solved_right)

    local_density = jnp.diagonal(full)[None]
    block_count = size // BLK
    picked = full.reshape(block_count, BLK, block_count, BLK)[
        block_list[0, :, 0], :, block_list[0, :, 1], :
    ]
    picked = picked.reshape(1, block_list.shape[1], BLK * BLK)
    regrouped = lax.all_to_all(picked, "energy", split_axis=1, concat_axis=0, tiled=True)
    result = self_energy(regrouped, derivative[0], pair_list)
    return (local_density, result[None])


def solution(mesh):
    placed = (
        P("cell", None, None),
        P("cell", None, None),
        P("cell", None, None),
        P("energy"),
        P("energy", None, None),
        P("cell", None, None),
        P("cell", "energy", None),
        P(),
    )
    return jax.shard_map(
        on_device,
        mesh=mesh,
        in_specs=placed,
        out_specs=(P("energy", "cell"), P("cell", "energy", None, None)),
        check_vma=False,
    )
```

time: 1140 us -> 779 us (0.68)
  waiting for transfers between devices: 505 us -> 0.68 us
  other arithmetic: 236 us -> 531 us
  starting transfers between devices: 265 us -> 94.3 us
  matrix products: 55.5 us -> 71.6 us
    ppermute x32 -> x26, waiting for transfers between devices: 505 us -> 0.07 us  [passed_along(): lax.ppermute(value, axis, [(source, source + steps) for source in range(f...]
    another operation x10 -> x54, other arithmetic: 45 us -> 337 us  [the longest x12 99.9 us: lower_solve(): return jax.scipy.linalg.solve_triangular(lower_factor, rhs, lower=True)]
    ppermute x32 -> x26, starting transfers between devices: 259 us -> 87.6 us  [passed_along(): lax.ppermute(value, axis, [(source, source + steps) for source in range(f...]
    dot_general x13 -> x47, matrix products: 10.2 us -> 28.6 us  [matmul(): return jnp.matmul(left_side, right_side, precision=lax.Precision.HIGHEST)]
  transfers between devices with their start and end apart: 33 -> 27, of which waited for: 32 -> 1; matrix products, arithmetic and copies ran while one was open for 1% -> 42% of each run, Pallas kernels for 0% -> 0%
where the time goes in v1:
time: 779 us; the launch traced here: 765 us
  other arithmetic  531 us (68%)
  starting transfers between devices  94.3 us (12%)
  matrix products  71.6 us (9%)
  local copies, waits for them, and re-layouts  59.7 us (8%)
    another operation x22, other arithmetic, invert(): lower_factor = jnp.linalg.cholesky(matrix)  124 us
    another operation x12, other arithmetic, lower_solve(): return jax.scipy.linalg.solve_triangular(lower_factor, rhs, lower=True)  99.9 us
    another operation x12, other arithmetic, combine(): root = jnp.linalg.cholesky(r_a)  94.7 us
    another operation x12, other arithmetic, combine(): root_reduced = jnp.linalg.cholesky(reduced)  94.4 us
    ppermute x26, starting transfers between devices, passed_along(): lax.ppermute(value, axis, [(source, source + steps) for source in range(f...  87.6 us
    another operation x3, other arithmetic, invert(): return jax.scipy.linalg.cho_solve((lower_factor, True), identity)  61.5 us
    dot_general x47, matrix products, matmul(): return jnp.matmul(left_side, right_side, precision=lax.Precision.HIGHEST)  28.6 us
    another operation x22, matrix products, invert(): return jax.scipy.linalg.cho_solve((lower_factor, True), identity)  26.9 us
  transfers between devices with their start and end apart: 27, of which 1 were waited for; matrix products, arithmetic and copies ran while one was open for 42% of the time, Pallas kernels for 0%

profile of v1, /device:TPU:97, one launch (start us, length us, event | category | flops | bytes accessed | tf_op | source)
XLA Modules:
  0.0 765.0 jit_solution(15902981191747677721)
XLA Ops:
  14.3 11.7 %cholesky.210 = f32[128,128]{1,0:T(8,128)S(1)} custom-call(f32[128,128]{1,0:T(8,128)S(1)} %copy.357), custom_call_target="Cholesky" | custom-call | tf_op jit(solution)/shard_map/jit(cholesky)/cholesky | solution.py:24
  26.3 9.8 %custom-call.59 = f32[1,128,128]{1,2,0:T(8,128)S(1)} custom-call(f32[1,128,128]{2,1,0:T(8,128)S(1)} %copy.360), custom_call_target="InvertDiagBlocksLowerTriangular" | custom-call | tf_op jit(solution)/shard_map/jit(cholesky)/cholesky | solution.py:24
  41.1 11.7 %cholesky.230 = f32[128,128]{1,0:T(8,128)S(1)} custom-call(f32[128,128]{1,0:T(8,128)S(1)} %copy.362), custom_call_target="Cholesky" | custom-call | tf_op jit(solution)/shard_map/jit(cholesky)/cholesky | solution.py:24
  53.3 10.1 %custom-call.60 = f32[1,128,128]{1,2,0:T(8,128)S(1)} custom-call(f32[1,128,128]{2,1,0:T(8,128)S(1)} %copy.368), custom_call_target="InvertDiagBlocksLowerTriangular" | custom-call | tf_op jit(solution)/shard_map/jit(cholesky)/cholesky | solution.py:24
  65.4 11.7 %cholesky.443 = f32[128,128]{1,0:T(8,128)S(1)} custom-call(f32[128,128]{1,0:T(8,128)S(1)} %copy.371), custom_call_target="Cholesky" | custom-call | tf_op jit(solution)/shard_map/jit(cholesky)/cholesky | solution.py:24
  77.5 9.8 %custom-call.61 = f32[1,128,128]{1,2,0:T(8,128)S(1)} custom-call(f32[1,128,128]{2,1,0:T(8,128)S(1)} %copy.375), custom_call_target="InvertDiagBlocksLowerTriangular" | custom-call | tf_op jit(solution)/shard_map/jit(cholesky)/cholesky | solution.py:24
  89.3 11.9 %cholesky.462 = f32[128,128]{1,0:T(8,128)S(1)} custom-call(f32[128,128]{1,0:T(8,128)S(1)} %copy.378), custom_call_target="Cholesky" | custom-call | tf_op jit(solution)/shard_map/jit(cholesky)/cholesky | solution.py:24
  101.5 9.8 %custom-call.62 = f32[1,128,128]{1,2,0:T(8,128)S(1)} custom-call(f32[1,128,128]{2,1,0:T(8,128)S(1)} %copy.382), custom_call_target="InvertDiagBlocksLowerTriangular" | custom-call | tf_op jit(solution)/shard_map/jit(cholesky)/cholesky | solution.py:24
  113.3 11.7 %cholesky.481 = f32[128,128]{1,0:T(8,128)S(1)} custom-call(f32[128,128]{1,0:T(8,128)S(1)} %copy.385), custom_call_target="Cholesky" | custom-call | tf_op jit(solution)/shard_map/jit(cholesky)/cholesky | solution.py:24
  125.3 9.8 %custom-call.63 = f32[1,128,128]{1,2,0:T(8,128)S(1)} custom-call(f32[1,128,128]{2,1,0:T(8,128)S(1)} %copy.389), custom_call_target="InvertDiagBlocksLowerTriangular" | custom-call | tf_op jit(solution)/shard_map/jit(cholesky)/cholesky | solution.py:24
  137.1 12.1 %cholesky.499 = f32[128,128]{1,0:T(8,128)S(1)} custom-call(f32[128,128]{1,0:T(8,128)S(1)} %copy.392), custom_call_target="Cholesky" | custom-call | tf_op jit(solution)/shard_map/jit(cholesky)/cholesky | solution.py:24
  158.0 21.5 %while.2 = (s32[]{:T(128)}, f32[768,768]{0,1:T(8,128)}, s32[6,2]{0,1:T(2,128)S(1)}, f32[6,128,128]{2,1,0:T(8,128)}, s32[]{:T(128)}) while((s32[]{:T(128)}, f32[768,768]{0,1:T(8,128)}, s32[6,2]{0,1:T(2,128)S(1)}, f32[6,128,128]{2,1,0:T(8,128)}, s32[]{:T(128)}) %tuple.69), condition=%wide.while_cond.1, body=%wide.while_body.1.sunk | while | flops 2 | bytes 393329 | solution.py:26
  179.5 59.9 %custom-call.64 = f32[6,128,128]{1,2,0:T(8,128)S(1)} custom-call(f32[6,128,128]{2,1,0:T(8,128)} %get-tuple-element.25), custom_call_target="InvertDiagBlocksLowerTriangular" | custom-call | tf_op jit(solution)/shard_map/jit(_cho_solve)/triangular_solve | solution.py:26
  252.1 3.6 convolution_subtract_fusion.3
  267.1 5.3 collective-permute-start.4
  274.5 4.9 collective-permute-start.1
  289.2 4.9 collective-permute-start.7
  294.3 23.7 %custom-call.82 = f32[2,128,128]{2,1,0:T(8,128)S(1)} custom-call(f32[2,128,128]{2,1,0:T(8,128)S(1)} %fusion.106), custom_call_target="Cholesky" | custom-call | tf_op jit(solution)/shard_map/jit(cholesky)/cholesky | solution.py:45
  320.0 23.5 %custom-call.83 = f32[2,128,128]{2,1,0:T(8,128)S(1)} custom-call(f32[2,128,128]{2,1,0:T(8,128)S(1)} %fusion.105), custom_call_target="Cholesky" | custom-call | tf_op jit(solution)/shard_map/jit(cholesky)/cholesky | solution.py:49
  343.7 20.1 %custom-call.84 = f32[2,1,128,128]{2,3,1,0:T(8,128)S(1)} custom-call(f32[2,1,128,128]{3,2,1,0:T(8,128)S(1)} %select_bitcast_fusion.3), custom_call_target="InvertDiagBlocksLowerTriangular" | custom-call | tf_op jit(solution)/shard_map/jit(_solve_triangular)/vmap()/triangular_solve | solution.py:30
  368.1 4.6 collective-permute-start.6
  374.7 3.4 collective-permute-start.9
  380.0 4.6 collective-permute-start.13
  384.7 23.5 %custom-call.85 = f32[2,128,128]{2,1,0:T(8,128)S(1)} custom-call(f32[2,128,128]{2,1,0:T(8,128)S(1)} %fusion.103), custom_call_target="Cholesky" | custom-call | tf_op jit(solution)/shard_map/jit(cholesky)/cholesky | solution.py:45
  409.4 23.5 %custom-call.86 = f32[2,128,128]{2,1,0:T(8,128)S(1)} custom-call(f32[2,128,128]{2,1,0:T(8,128)S(1)} %fusion.102), custom_call_target="Cholesky" | custom-call | tf_op jit(solution)/shard_map/jit(cholesky)/cholesky | solution.py:49
  433.5 19.9 %custom-call.87 = f32[2,1,128,128]{2,3,1,0:T(8,128)S(1)} custom-call(f32[2,1,128,128]{3,2,1,0:T(8,128)S(1)} %select_bitcast_fusion.2), custom_call_target="InvertDiagBlocksLowerTriangular" | custom-call | tf_op jit(solution)/shard_map/jit(_solve_triangular)/vmap()/triangular_solve | solution.py:30
  457.9 5.5 collective-permute-start.12
  465.4 4.3 collective-permute-start.15
  471.6 5.5 collective-permute-start.19
  477.2 23.5 %custom-call.88 = f32[2,128,128]{2,1,0:T(8,128)S(1)} custom-call(f32[2,128,128]{2,1,0:T(8,128)S(1)} %fusion.100), custom_call_target="Cholesky" | custom-call | tf_op jit(solution)/shard_map/jit(cholesky)/cholesky | solution.py:45
  501.9 23.5 %custom-call.89 = f32[2,128,128]{2,1,0:T(8,128)S(1)} custom-call(f32[2,128,128]{2,1,0:T(8,128)S(1)} %fusion.99), custom_call_target="Cholesky" | custom-call | tf_op jit(solution)/shard_map/jit(cholesky)/cholesky | solution.py:49
  526.0 20.1 %custom-call.90 = f32[2,1,128,128]{2,3,1,0:T(8,128)S(1)} custom-call(f32[2,1,128,128]{3,2,1,0:T(8,128)S(1)} %select_bitcast_fusion.1), custom_call_target="InvertDiagBlocksLowerTriangular" | custom-call | tf_op jit(solution)/shard_map/jit(_solve_triangular)/vmap()/triangular_solve | solution.py:30
  550.0 7.9 %collective-permute-start.18 = (f32[128,128]{0,1:T(8,128)S(1)}, f32[128,128]{0,1:T(8,128)S(1)}, u32[]{:S(2)}, u32[]{:S(2)}) collective-permute-start(f32[128,128]{0,1:T(8,128)S(1)} %get-tuple-element.69), channel_id=1, source_target_pairs={{0,128},{16,144},{32,160},{48,176},{64,192},{80,208},{96,224},{112... | collective-permute-start | bytes 196616 | tf_op jit(solution)/shard_map/ppermute | solution.py:12
  561.8 8.5 %collective-permute-start.24 = (f32[128,128]{0,1:T(8,128)S(1)}, f32[128,128]{0,1:T(8,128)}, u32[]{:S(2)}, u32[]{:S(2)}) collective-permute-start(f32[128,128]{0,1:T(8,128)S(1)} %get-tuple-element.70), channel_id=1, source_target_pairs={{0,128},{16,144},{32,160},{48,176},{64,192},{80,208},{96,224},{112... | collective-permute-start | bytes 196616 | tf_op jit(solution)/shard_map/ppermute | solution.py:12
  570.5 23.5 %custom-call.91 = f32[2,128,128]{2,1,0:T(8,128)S(1)} custom-call(f32[2,128,128]{2,1,0:T(8,128)S(1)} %fusion.97), custom_call_target="Cholesky" | custom-call | tf_op jit(solution)/shard_map/jit(cholesky)/cholesky | solution.py:45
  595.2 23.5 %custom-call.92 = f32[2,128,128]{2,1,0:T(8,128)S(1)} custom-call(f32[2,128,128]{2,1,0:T(8,128)S(1)} %fusion.96), custom_call_target="Cholesky" | custom-call | tf_op jit(solution)/shard_map/jit(cholesky)/cholesky | solution.py:49
  619.3 19.8 %custom-call.93 = f32[2,1,128,128]{2,3,1,0:T(8,128)S(1)} custom-call(f32[2,1,128,128]{3,2,1,0:T(8,128)S(1)} %select_bitcast_fusion), custom_call_target="InvertDiagBlocksLowerTriangular" | custom-call | tf_op jit(solution)/shard_map/jit(_solve_triangular)/vmap()/triangular_solve | solution.py:30
  643.4 4.1 collective-permute-start.25
  647.7 23.5 %custom-call.94 = f32[2,128,128]{2,1,0:T(8,128)S(1)} custom-call(f32[2,128,128]{2,1,0:T(8,128)S(1)} %fusion.94), custom_call_target="Cholesky" | custom-call | tf_op jit(solution)/shard_map/jit(cholesky)/cholesky | solution.py:121
  674.2 23.7 %custom-call.95 = f32[2,128,128]{2,1,0:T(8,128)S(1)} custom-call(f32[2,128,128]{2,1,0:T(8,128)S(1)} %fusion.93), custom_call_target="Cholesky" | custom-call | tf_op jit(solution)/shard_map/jit(cholesky)/cholesky | solution.py:127
  698.2 9.8 %custom-call.96 = f32[1,128,128]{1,2,0:T(8,128)S(1)} custom-call(f32[1,128,128]{2,1,0:T(8,128)S(1)} %get-tuple-element.65), custom_call_target="InvertDiagBlocksLowerTriangular" | custom-call | tf_op jit(solution)/shard_map/jit(_solve_triangular)/triangular_solve | solution.py:30
  711.2 3.4 fusion.52
  715.1 9.8 %custom-call.97 = f32[1,128,128]{1,2,0:T(8,128)S(1)} custom-call(f32[1,128,128]{2,1,0:T(8,128)S(1)} %get-tuple-element.64), custom_call_target="InvertDiagBlocksLowerTriangular" | custom-call | tf_op jit(solution)/shard_map/jit(_solve_triangular)/triangular_solve | solution.py:30
  725.5 4.8 add_add_fusion
  730.3 3.6 reshape.272
  733.9 6.4 copy.482
  744.3 6.8 all-to-all-start
  751.1 6.3 gather_fusion
  (351 shorter events, 144.5 us)
Async XLA Ops:
  0.6 7.7 %copy-start = (f32[1,128,128]{2,1,0:T(8,128)S(1)}, f32[1,128,128]{2,1,0:T(8,128)}, u32[]{:S(2)}) copy-start(f32[1,128,128]{2,1,0:T(8,128)} %param.21) | copy-start | bytes 196612
  6.4 1.9 copy-start.15
  12.8 1.4 copy-start.7
  179.5 63.6 %copy-start.3 = (f32[768,768]{0,1:T(8,128)S(1)}, f32[768,768]{0,1:T(8,128)}, u32[]{:S(2)}) copy-start(f32[768,768]{0,1:T(8,128)} %get-tuple-element.158) | copy-start | bytes 7077892
  239.5 16.3 %copy-start.12 = (f32[6,128,128]{1,2,0:T(8,128)}, f32[6,128,128]{1,2,0:T(8,128)S(1)}, u32[]{:S(2)}) copy-start(f32[6,128,128]{1,2,0:T(8,128)S(1)} %custom-call.64) | copy-start | bytes 1179652
  242.6 3.7 copy-start.4
  256.2 3.8 copy-start.13
  260.5 3.6 copy-start.5
  261.9 2.3 copy-start.9
  265.6 18.4 %copy-start.11 = (f32[128,768]{1,0:T(8,128)S(1)}, f32[128,768]{1,0:T(8,128)}, u32[]{:S(2)}) copy-start(f32[128,768]{1,0:T(8,128)} %get-tuple-element.107) | copy-start | bytes 1179652
  265.6 19.2 %copy-start.10 = (f32[128,768]{1,0:T(8,128)S(1)}, f32[128,768]{1,0:T(8,128)}, u32[]{:S(2)}) copy-start(f32[128,768]{1,0:T(8,128)} %copy-done.9) | copy-start | bytes 1179652
  265.6 20.0 %copy-start.6 = (f32[128,768]{1,0:T(8,128)S(1)}, f32[128,768]{1,0:T(8,128)}, u32[]{:S(2)}) copy-start(f32[128,768]{1,0:T(8,128)} %copy-done.5) | copy-start | bytes 1179652
  266.8 21.1 %copy-start.14 = (f32[128,768]{1,0:T(8,128)}, f32[128,768]{1,0:T(8,128)S(1)}, u32[]{:S(2)}) copy-start(f32[128,768]{1,0:T(8,128)S(1)} %get-tuple-element.109) | copy-start | bytes 1179652
  267.1 51.9 %collective-permute-start.4 = (f32[128,128]{1,0:T(8,128)S(1)}, f32[128,128]{1,0:T(8,128)S(1)}, u32[]{:S(2)}, u32[]{:S(2)}) collective-permute-start(f32[128,128]{1,0:T(8,128)S(1)} %fusion.151), channel_id=1, source_target_pairs={{0,16},{16,32},{32,48},{48,64},{64,80},{80,96},{96,112},{112,128},... | collective-permute-start | bytes 196616 | tf_op jit(solution)/shard_map/ppermute | solution.py:12
  272.4 46.1 %collective-permute-start.3 = (f32[128,128]{1,0:T(8,128)S(1)}, f32[128,128]{1,0:T(8,128)S(1)}, u32[]{:S(2)}, u32[]{:S(2)}) collective-permute-start(f32[128,128]{1,0:T(8,128)S(1)} %fusion.151), channel_id=1, source_target_pairs={{16,0},{32,16},{48,32},{64,48},{80,64},{96,80},{112,96},{128,112},... | collective-permute-start | bytes 196616 | tf_op jit(solution)/shard_map/ppermute | solution.py:12
  274.4 13.5 %copy-start.18 = (s32[1,16,2]{1,2,0:T(2,128)S(1)}, s32[1,16,2]{1,2,0:T(2,128)}, u32[]{:S(2)}) copy-start(s32[1,16,2]{1,2,0:T(2,128)} %param.22) | copy-start | bytes 388
  274.4 14.0 %copy-start.16 = (f32[1,1,4096]{2,1,0:T(1,128)S(1)}, f32[1,1,4096]{2,1,0:T(1,128)}, u32[]{:S(2)}) copy-start(f32[1,1,4096]{2,1,0:T(1,128)} %param.23) | copy-start | bytes 49156
  274.5 14.7 %collective-permute-start.1 = (f32[128,128]{0,1:T(8,128)S(1)}, f32[128,128]{0,1:T(8,128)S(1)}, u32[]{:S(2)}, u32[]{:S(2)}) collective-permute-start(f32[128,128]{0,1:T(8,128)S(1)} %copy.562), channel_id=1, source_target_pairs={{0,16},{16,32},{32,48},{48,64},{64,80},{80,96},{96,112},{112,128},... | collective-permute-start | bytes 196616 | tf_op jit(solution)/shard_map/ppermute | solution.py:12
  279.4 86.0 %collective-permute-start = (f32[128,128]{0,1:T(8,128)S(1)}, f32[128,128]{0,1:T(8,128)S(1)}, u32[]{:S(2)}, u32[]{:S(2)}) collective-permute-start(f32[128,128]{0,1:T(8,128)S(1)} %copy.562), channel_id=1, source_target_pairs={{16,0},{32,16},{48,32},{64,48},{80,64},{96,80},{112,96},{128,112},... | collective-permute-start | bytes 196616 | tf_op jit(solution)/shard_map/ppermute | solution.py:12
  281.9 36.2 %collective-permute-start.2 = (f32[128,128]{0,1:T(8,128)S(1)}, f32[128,128]{0,1:T(8,128)S(1)}, u32[]{:S(2)}, u32[]{:S(2)}) collective-permute-start(f32[128,128]{0,1:T(8,128)S(1)} %fusion.317), channel_id=1, source_target_pairs={{16,0},{32,16},{48,32},{64,48},{80,64},{96,80},{112,96},{128,112},... | collective-permute-start | bytes 196616 | tf_op jit(solution)/shard_map/ppermute | solution.py:12
  289.2 76.5 %collective-permute-start.7 = (f32[128,128]{0,1:T(8,128)S(1)}, f32[128,128]{0,1:T(8,128)S(1)}, u32[]{:S(2)}, u32[]{:S(2)}) collective-permute-start(f32[128,128]{0,1:T(8,128)S(1)} %fusion.317), channel_id=1, source_target_pairs={{0,16},{16,32},{32,48},{48,64},{64,80},{80,96},{96,112},{112,128},... | collective-permute-start | bytes 196616 | tf_op jit(solution)/shard_map/ppermute | solution.py:12
  366.2 42.1 %collective-permute-start.8 = (f32[128,128]{0,1:T(8,128)S(1)}, f32[128,128]{0,1:T(8,128)S(1)}, u32[]{:S(2)}, u32[]{:S(2)}) collective-permute-start(f32[128,128]{0,1:T(8,128)S(1)} %get-tuple-element.63), channel_id=1, source_target_pairs={{32,0},{48,16},{64,32},{80,48},{96,64},{112,80},{128,96},{144,112}... | collective-permute-start | bytes 196616 | tf_op jit(solution)/shard_map/ppermute | solution.py:12
  368.1 11.8 %collective-permute-start.6 = (f32[128,128]{0,1:T(8,128)S(1)}, f32[128,128]{0,1:T(8,128)S(1)}, u32[]{:S(2)}, u32[]{:S(2)}) collective-permute-start(f32[128,128]{0,1:T(8,128)S(1)} %get-tuple-element.61), channel_id=1, source_target_pairs={{0,32},{16,48},{32,64},{48,80},{64,96},{80,112},{96,128},{112,144}... | collective-permute-start | bytes 196616 | tf_op jit(solution)/shard_map/ppermute | solution.py:12
  372.8 60.4 %collective-permute-start.10 = (f32[128,128]{0,1:T(8,128)S(1)}, f32[128,128]{0,1:T(8,128)S(1)}, u32[]{:S(2)}, u32[]{:S(2)}) collective-permute-start(f32[128,128]{0,1:T(8,128)S(1)} %get-tuple-element.58), channel_id=1, source_target_pairs={{0,32},{16,48},{32,64},{48,80},{64,96},{80,112},{96,128},{112,144}... | collective-permute-start | bytes 196616 | tf_op jit(solution)/shard_map/ppermute | solution.py:12
  374.7 78.7 %collective-permute-start.9 = (f32[128,128]{0,1:T(8,128)S(1)}, f32[128,128]{0,1:T(8,128)S(1)}, u32[]{:S(2)}, u32[]{:S(2)}) collective-permute-start(f32[128,128]{0,1:T(8,128)S(1)} %get-tuple-element.59), channel_id=1, source_target_pairs={{32,0},{48,16},{64,32},{80,48},{96,64},{112,80},{128,96},{144,112}... | collective-permute-start | bytes 196616 | tf_op jit(solution)/shard_map/ppermute | solution.py:12
  378.1 77.1 %collective-permute-start.5 = (f32[128,128]{0,1:T(8,128)S(1)}, f32[128,128]{0,1:T(8,128)S(1)}, u32[]{:S(2)}, u32[]{:S(2)}) collective-permute-start(f32[128,128]{0,1:T(8,128)S(1)} %get-tuple-element.60), channel_id=1, source_target_pairs={{32,0},{48,16},{64,32},{80,48},{96,64},{112,80},{128,96},{144,112}... | collective-permute-start | bytes 196616 | tf_op jit(solution)/shard_map/ppermute | solution.py:12
  380.0 75.6 %collective-permute-start.13 = (f32[128,128]{0,1:T(8,128)S(1)}, f32[128,128]{0,1:T(8,128)S(1)}, u32[]{:S(2)}, u32[]{:S(2)}) collective-permute-start(f32[128,128]{0,1:T(8,128)S(1)} %get-tuple-element.62), channel_id=1, source_target_pairs={{0,32},{16,48},{32,64},{48,80},{64,96},{80,112},{96,128},{112,144}... | collective-permute-start | bytes 196616 | tf_op jit(solution)/shard_map/ppermute | solution.py:12
  456.0 44.8 %collective-permute-start.14 = (f32[128,128]{0,1:T(8,128)S(1)}, f32[128,128]{0,1:T(8,128)S(1)}, u32[]{:S(2)}, u32[]{:S(2)}) collective-permute-start(f32[128,128]{0,1:T(8,128)S(1)} %get-tuple-element.77), channel_id=1, source_target_pairs={{64,0},{80,16},{96,32},{112,48},{128,64},{144,80},{160,96},{176,11... | collective-permute-start | bytes 196616 | tf_op jit(solution)/shard_map/ppermute | solution.py:12
  457.9 13.6 %collective-permute-start.12 = (f32[128,128]{0,1:T(8,128)S(1)}, f32[128,128]{0,1:T(8,128)S(1)}, u32[]{:S(2)}, u32[]{:S(2)}) collective-permute-start(f32[128,128]{0,1:T(8,128)S(1)} %get-tuple-element.75), channel_id=1, source_target_pairs={{0,64},{16,80},{32,96},{48,112},{64,128},{80,144},{96,160},{112,17... | collective-permute-start | bytes 196616 | tf_op jit(solution)/shard_map/ppermute | solution.py:12
  463.4 62.2 %collective-permute-start.16 = (f32[128,128]{0,1:T(8,128)S(1)}, f32[128,128]{0,1:T(8,128)S(1)}, u32[]{:S(2)}, u32[]{:S(2)}) collective-permute-start(f32[128,128]{0,1:T(8,128)S(1)} %get-tuple-element.72), channel_id=1, source_target_pairs={{0,64},{16,80},{32,96},{48,112},{64,128},{80,144},{96,160},{112,17... | collective-permute-start | bytes 196616 | tf_op jit(solution)/shard_map/ppermute | solution.py:12
  465.4 80.7 %collective-permute-start.15 = (f32[128,128]{0,1:T(8,128)S(1)}, f32[128,128]{0,1:T(8,128)S(1)}, u32[]{:S(2)}, u32[]{:S(2)}) collective-permute-start(f32[128,128]{0,1:T(8,128)S(1)} %get-tuple-element.73), channel_id=1, source_target_pairs={{64,0},{80,16},{96,32},{112,48},{128,64},{144,80},{160,96},{176,11... | collective-permute-start | bytes 196616 | tf_op jit(solution)/shard_map/ppermute | solution.py:12
  469.6 78.2 %collective-permute-start.11 = (f32[128,128]{0,1:T(8,128)S(1)}, f32[128,128]{0,1:T(8,128)S(1)}, u32[]{:S(2)}, u32[]{:S(2)}) collective-permute-start(f32[128,128]{0,1:T(8,128)S(1)} %get-tuple-element.74), channel_id=1, source_target_pairs={{64,0},{80,16},{96,32},{112,48},{128,64},{144,80},{160,96},{176,11... | collective-permute-start | bytes 196616 | tf_op jit(solution)/shard_map/ppermute | solution.py:12
  471.6 76.7 %collective-permute-start.19 = (f32[128,128]{0,1:T(8,128)S(1)}, f32[128,128]{0,1:T(8,128)S(1)}, u32[]{:S(2)}, u32[]{:S(2)}) collective-permute-start(f32[128,128]{0,1:T(8,128)S(1)} %get-tuple-element.76), channel_id=1, source_target_pairs={{0,64},{16,80},{32,96},{48,112},{64,128},{80,144},{96,160},{112,17... | collective-permute-start | bytes 196616 | tf_op jit(solution)/shard_map/ppermute | solution.py:12
  548.7 45.4 %collective-permute-start.20 = (f32[128,128]{0,1:T(8,128)S(1)}, f32[128,128]{0,1:T(8,128)S(1)}, u32[]{:S(2)}, u32[]{:S(2)}) collective-permute-start(f32[128,128]{0,1:T(8,128)S(1)} %get-tuple-element.71), channel_id=1, source_target_pairs={{128,0},{144,16},{160,32},{176,48},{192,64},{208,80},{224,96},{240... | collective-permute-start | bytes 196616 | tf_op jit(solution)/shard_map/ppermute | solution.py:12
  550.0 11.8 %collective-permute-start.18 = (f32[128,128]{0,1:T(8,128)S(1)}, f32[128,128]{0,1:T(8,128)S(1)}, u32[]{:S(2)}, u32[]{:S(2)}) collective-permute-start(f32[128,128]{0,1:T(8,128)S(1)} %get-tuple-element.69), channel_id=1, source_target_pairs={{0,128},{16,144},{32,160},{48,176},{64,192},{80,208},{96,224},{112... | collective-permute-start | bytes 196616 | tf_op jit(solution)/shard_map/ppermute | solution.py:12
  557.9 61.0 %collective-permute-start.22 = (f32[128,128]{0,1:T(8,128)S(1)}, f32[128,128]{0,1:T(8,128)S(1)}, u32[]{:S(2)}, u32[]{:S(2)}) collective-permute-start(f32[128,128]{0,1:T(8,128)S(1)} %get-tuple-element.66), channel_id=1, source_target_pairs={{0,128},{16,144},{32,160},{48,176},{64,192},{80,208},{96,224},{112... | collective-permute-start | bytes 196616 | tf_op jit(solution)/shard_map/ppermute | solution.py:12
  559.2 79.9 %collective-permute-start.21 = (f32[128,128]{0,1:T(8,128)S(1)}, f32[128,128]{0,1:T(8,128)S(1)}, u32[]{:S(2)}, u32[]{:S(2)}) collective-permute-start(f32[128,128]{0,1:T(8,128)S(1)} %get-tuple-element.67), channel_id=1, source_target_pairs={{128,0},{144,16},{160,32},{176,48},{192,64},{208,80},{224,96},{240... | collective-permute-start | bytes 196616 | tf_op jit(solution)/shard_map/ppermute | solution.py:12
  560.5 80.5 %collective-permute-start.17 = (f32[128,128]{0,1:T(8,128)S(1)}, f32[128,128]{0,1:T(8,128)S(1)}, u32[]{:S(2)}, u32[]{:S(2)}) collective-permute-start(f32[128,128]{0,1:T(8,128)S(1)} %get-tuple-element.68), channel_id=1, source_target_pairs={{128,0},{144,16},{160,32},{176,48},{192,64},{208,80},{224,96},{240... | collective-permute-start | bytes 196616 | tf_op jit(solution)/shard_map/ppermute | solution.py:12
  561.8 81.5 %collective-permute-start.24 = (f32[128,128]{0,1:T(8,128)S(1)}, f32[128,128]{0,1:T(8,128)}, u32[]{:S(2)}, u32[]{:S(2)}) collective-permute-start(f32[128,128]{0,1:T(8,128)S(1)} %get-tuple-element.70), channel_id=1, source_target_pairs={{0,128},{16,144},{32,160},{48,176},{64,192},{80,208},{96,224},{112... | collective-permute-start | bytes 196616 | tf_op jit(solution)/shard_map/ppermute | solution.py:12
  640.0 31.7 %copy-start.8 = (f32[768,768]{1,0:T(8,128)S(1)}, f32[768,768]{1,0:T(8,128)}, u32[]{:S(2)}) copy-start(f32[768,768]{1,0:T(8,128)} %constant_dynamic-update-slice_fusion.10) | copy-start | bytes 7077892
  641.1 6.4 collective-permute-start.23
  643.4 29.8 %collective-permute-start.25 = (f32[128,128]{0,1:T(8,128)S(1)}, f32[128,128]{0,1:T(8,128)S(1)}, u32[]{:S(2)}, u32[]{:S(2)}) collective-permute-start(f32[128,128]{0,1:T(8,128)S(1)} %fusion.130), channel_id=1, source_target_pairs={{16,0},{32,16},{48,32},{64,48},{80,64},{96,80},{112,96},{128,112},... | collective-permute-start | bytes 196616 | tf_op jit(solution)/shard_map/ppermute | solution.py:12
  710.6 4.5 copy-start.2
  740.3 10.7 %copy-start.17 = (s32[16,2]{0,1:T(2,128)S(1)}, s32[16,2]{0,1:T(2,128)}, u32[]{:S(2)}) copy-start(s32[16,2]{0,1:T(2,128)} %param.24) | copy-start | bytes 388
  744.3 14.3 %all-to-all-start = ((f32[1,16,4096]{2,0,1:T(1,128)}), f32[1,16,4096]{2,0,1:T(1,128)S(1)}, u32[]{:S(2)}, u32[]{:S(2)}) async-start(f32[1,16,4096]{2,0,1:T(1,128)} %reshape.342), calls=%async_computation | async-start | bytes 524288 | tf_op jit(solution)/shard_map/all_to_all | solution.py:142
  761.7 2.8 copy-start.1
